TPU v7x, 32 devices: a whole 2x2x4 slice. The times are simulated.
32 devices in a mesh: grp: 2 (over y), tm: 4 (over z), height: 4 (over x, core).
Axes of the slice: x: 2, y: 2, z: 4, core: 2. Of those that a mesh axis runs over, the one named last changes fastest.
Arguments:
- latents: bfloat16 [8, 8, 160, 384], P(('grp', 'tm'), 'height'), parts along dimension 0, may hold values from -6 to 6
- gain: float32 [384], replicated, may hold values from 0.1 to 1.9
- bias: float32 [384], replicated, may hold values from -3 to 3
- weight: bfloat16 [10368, 384], replicated, may hold values from -0.0625 to 0.0625
- cotangent: bfloat16 [8, 8, 160, 384], P(('grp', 'tm'), 'height'), parts along dimension 0, may hold values from -6 to 6
Outputs:
- output: bfloat16 [8, 8, 160, 384], P(('grp', 'tm'), 'height'), parts along dimension 0
- latent_grad: bfloat16 [8, 8, 160, 384], P(('grp', 'tm'), 'height'), parts along dimension 0
- weight_grad: float32 [20736, 384], P(('grp', 'tm'), 'height'), parts along dimension 0
There are 2 independent parts, one for each index of `grp`. A program takes and returns all parts, laid end to end along the dimension named above; an argument that names none is the same for every part. Nothing has to cross between parts.
All inputs are finite; a program needn't handle non-finite values.
Results may differ from a plain program's by a relative error of at most 0.0029.
Values may be sent and summed in bfloat16 or wider, within the bound.
No kernel may reach another device: no remote copies, remote signals or barrier semaphores. Data moves between devices by JAX's collectives and lax.ppermute only.
A program may use at most 128 MiB of HBM per device.

v0:
```python
import math
import jax
import jax.numpy as jnp
from jax import lax
from jax.sharding import PartitionSpec as P


def shifted_2(value, axis, by):
    devices = lax.axis_size(axis)
    pairs = [(i, i + by) for i in range(devices) if 0 <= i + by < devices]
    return lax.ppermute(value, axis, pairs)


def padded(cells, sides, width):
    for axis, dim in sides:
        count = lax.axis_size(axis)
        ends = count - 1
        head = lax.slice_in_dim(cells, 0, width, axis=dim)
        tail = lax.slice_in_dim(cells, cells.shape[dim] - width, cells.shape[dim], axis=dim)
        cells = jnp.concatenate(
            [
                lax.ppermute(tail, axis, [(i, (i + 1) % count) for i in range(ends)]),
                cells,
                lax.ppermute(head, axis, [((i + 1) % count, i) for i in range(ends)]),
            ],
            axis=dim,
        )
    return cells


def forward_arrange(cube):
    depth, rows_t, cols_t, inputs, outputs = cube.shape
    return cube.transpose(0, 1, 3, 2, 4).reshape(9, inputs, 3 * outputs)


def backward_arrange(cube):
    depth, rows_t, cols_t, inputs, outputs = cube.shape
    return cube.transpose(0, 1, 4, 2, 3).reshape(9, outputs, 3 * inputs)


def forward_conv(window, cube, row_total, col_total):
    window = window[:, :, : col_total + 2]
    result = lax.conv_general_dilated(
        window[None],
        cube,
        (1, 1, 1),
        "VALID",
        dimension_numbers=("NDHWC", "DHWIO", "NDHWC"),
        preferred_element_type=jnp.float32,
    )
    return result[0, 0]


def backward_conv(window, cube, row_total, col_total):
    window = window[:, :, : col_total + 2]
    result = lax.conv_general_dilated(
        window[None],
        jnp.flip(cube, (0, 1, 2)),
        (1, 1, 1),
        "VALID",
        dimension_numbers=("NDHWC", "DHWOI", "NDHWC"),
        preferred_element_type=jnp.float32,
    )
    return result[0, 0]


def pair_count(tap_rows, share_rows, pair_rows, parts):
    most = 1
    for index in range(parts):
        first = index * share_rows
        last = first + share_rows - 1
        most = max(most, last // pair_rows - first // pair_rows + 1)
    return most


def depth_span(share_rows, tap_rows, channels):
    plane_rows = 9 * channels
    most = 1
    for index in range(tap_rows // share_rows):
        first = index * share_rows
        last = first + share_rows - 1
        most = max(most, last // plane_rows - first // plane_rows + 1)
    return most


def block_weight_grad(framed, cot_all, frame_index, share_rows, channels):
    frame_total, row_total, col_total, slots = cot_all.shape
    plane_rows = 9 * channels
    tap_rows = 27 * channels
    span = depth_span(share_rows, tap_rows, channels)
    first_row = frame_index * share_rows
    first_depth = jnp.minimum(first_row // plane_rows, 3 - span)
    frames = lax.dynamic_slice_in_dim(framed, first_depth, frame_total + span - 1, 0)
    frames = frames[:, :, : col_total + 2]
    terms = lax.conv_general_dilated(
        frames[..., None],
        cot_all[:, :, :, None, :],
        (1, 1, 1),
        "VALID",
        dimension_numbers=("DHWNC", "DHWIO", "DHWNC"),
        preferred_element_type=jnp.float32,
    ).reshape(span * plane_rows, slots)
    return lax.dynamic_slice_in_dim(terms, first_row - first_depth * plane_rows, share_rows, 0)


def gather_rows(own, height_count):
    frame_total, row_count, col_count, channels = own.shape
    height_index = lax.axis_index("height")
    core = height_index % 2
    chip = height_index // 2
    chips = height_count // 2
    first = core == 0
    sibling = [(i, i ^ 1) for i in range(height_count)]
    mine = [own] + [
        lax.ppermute(
            own, "height", [(i, (i + 2 * step) % height_count) for i in range(height_count)]
        )
        for step in range(1, chips)
    ]
    stacked = jnp.concatenate(mine, axis=1)
    twins = lax.ppermute(stacked, "height", sibling)
    block = 2 * row_count
    relative = []
    for step in reversed(range(chips)):
        ours = stacked[:, step * row_count : (step + 1) * row_count]
        theirs = twins[:, step * row_count : (step + 1) * row_count]
        relative.append(
            jnp.where(
                first,
                jnp.concatenate([ours, theirs], axis=1),
                jnp.concatenate([theirs, ours], axis=1),
            )
        )
    relative = jnp.concatenate(relative, axis=1)
    return jnp.concatenate(
        [
            lax.dynamic_slice_in_dim(relative, (place - chip - 1) % chips * block, block, 1)
            for place in range(chips)
        ],
        axis=1,
    )


def local(latents, gain, bias, weight, cotangent):
    frame_count, row_count, col_count, channels = latents.shape
    latent_wide = latents.astype(jnp.float32)
    root_mean = jnp.sqrt(jnp.mean(latent_wide * latent_wide, axis=-1, keepdims=True) + 1e-06)
    normed = latent_wide / root_mean * gain
    hidden = jax.nn.silu(normed).astype(jnp.bfloat16)
    height_count = lax.axis_size("height")
    frame_devices = lax.axis_size("tm")
    frame_index = lax.axis_index("tm")
    row_index = lax.axis_index("height")
    total_rows = row_count * height_count
    total_frames = frame_count * frame_devices
    tap_rows = 27 * channels
    share_rows = tap_rows // frame_devices
    padded_cols = col_count + 2
    right_pad = padded_cols - col_count - 1
    inverse_root = 1.0 / math.sqrt(total_frames * total_rows * col_count)
    weight_cube = weight.reshape(3, 3, 3, channels, channels)
    both_frames = lax.all_gather(
        jnp.concatenate([hidden, cotangent], axis=-1), "tm", axis=0, tiled=True
    )
    hidden_all = gather_rows(both_frames[..., :channels], height_count)
    framed = jnp.pad(hidden_all, ((2, 0), (1, 1), (1, right_pad), (0, 0)))
    cot_frames = both_frames[..., channels:]
    cot_all = lax.all_to_all(cot_frames, "height", split_axis=3, concat_axis=1, tiled=True)
    window = lax.dynamic_slice(
        framed,
        (frame_index * frame_count, row_index * row_count, 0, 0),
        (frame_count + 2, row_count + 2, padded_cols, channels),
    )
    conv_out = forward_conv(window, weight_cube, row_count, col_count).reshape(
        frame_count, row_count, col_count, channels
    )
    output = (latent_wide + conv_out + bias).astype(jnp.bfloat16)
    weight_grad = (
        block_weight_grad(framed, cot_all, frame_index, share_rows, channels) * inverse_root
    )
    cot_future = lax.dynamic_slice_in_dim(
        jnp.pad(cot_frames, ((0, 2), (0, 0), (0, 0), (0, 0))), frame_index * frame_count, 3, 0
    )
    cotangent_edged = padded(cot_future, (("height", 1),), 1)
    future_block = jnp.pad(cotangent_edged, ((0, 0), (0, 0), (1, right_pad), (0, 0)))
    hidden_grad = backward_conv(future_block, weight_cube, row_count, col_count).reshape(
        frame_count, row_count, col_count, channels
    )
    sigmoid_pre = jax.nn.sigmoid(normed)
    normed_grad = hidden_grad * sigmoid_pre * (1.0 + normed * (1.0 - sigmoid_pre))
    scaled_grad = normed_grad * gain
    unit_latent = latent_wide / root_mean
    inner = jnp.mean(scaled_grad * unit_latent, axis=-1, keepdims=True)
    latent_grad = (
        cotangent.astype(jnp.float32) + (scaled_grad - unit_latent * inner) / root_mean
    ).astype(jnp.bfloat16)
    return (output, latent_grad, weight_grad)


def solution(mesh):
    placed = (
        P(("grp", "tm"), "height", None, None),
        P(),
        P(),
        P(),
        P(("grp", "tm"), "height", None, None),
    )
    return jax.shard_map(
        local,
        mesh=mesh,
        in_specs=placed,
        out_specs=(
            P(("grp", "tm"), "height", None, None),
            P(("grp", "tm"), "height", None, None),
            P(("grp", "tm"), "height"),
        ),
        check_vma=False,
    )
```

profile of v0, /device:TPU:0, one launch (start us, length us, event | category | flops | bytes accessed | tf_op | source)
XLA Modules:
  0.0 224.5 jit_solution(6320341675211582955)
XLA Ops:
  7.2 1.1 fusion.49
  8.3 1.2 multiply_convert_fusion
  9.5 1.8 pad_maximum_fusion.3
  11.3 46.4 %all-gather.2.cloned.1.call-done = bf16[4,2,160,768]{3,2,1,0:T(8,128)(2,1)} async-done(((bf16[1,2,160,768]{3,2,1,0:T(8,128)(2,1)}), bf16[4,2,160,768]{3,2,1,0:T(8,128)(2,1)}) %all-gather.2.cloned.1.call-update) | async-done | bytes 1966096 | tf_op jit(solution)/shard_map/all_gather | solution.py:162
  57.7 1.7 fusion.61
  59.4 1.5 collective-permute-start
  61.0 1.0 pad_dynamic-slice_fusion.5
  62.0 1.3 collective-permute-start.3
  63.3 3.8 %collective-permute-start.2 = (bf16[3,1,160,384]{3,2,1,0:T(8,128)(2,1)}, bf16[3,1,160,384]{3,2,1,0:T(8,128)(2,1)}, u32[]{:S(2)}, u32[]{:S(2)}) collective-permute-start(bf16[3,1,160,384]{3,2,1,0:T(8,128)(2,1)} %get-tuple-element.21), channel_id=1, source_target_pairs={{0,1},{1,2},{2,3},{4,5},{5,6},{6,7},{8,9},{9,10},{10,11},{12,13},{... | collective-permute-start | bytes 1105928 | tf_op jit(solution)/shard_map/ppermute | solution.py:22
  67.1 16.1 %collective-permute-done = bf16[4,2,160,384]{3,2,1,0:T(8,128)(2,1)S(1)} collective-permute-done((bf16[4,2,160,384]{3,2,1,0:T(8,128)(2,1)S(1)}, bf16[4,2,160,384]{3,2,1,0:T(8,128)(2,1)S(1)}, u32[]{:S(2)}, u32[]{:S(2)}) %collective-permute-start) | collective-permute-done | bytes 983072 | tf_op jit(solution)/shard_map/ppermute | solution.py:115
  83.1 1.6 pad_maximum_fusion.1
  84.8 2.5 %copy.92 = bf16[4,2,160,384]{2,0,1,3:T(4,128)(2,1)} copy(bf16[4,2,160,384]{3,2,1,0:T(8,128)(2,1)S(1)} %get-tuple-element.17) | data formatting | bytes 1966080 | tf_op jit(solution)/shard_map/slice | solution.py:167
  87.3 3.9 %all-to-all-start = ((bf16[4,2,160,384]{2,0,1,3:T(4,128)(2,1)}), bf16[4,2,160,384]{2,0,1,3:T(4,128)(2,1)S(1)}, u32[]{:S(2)}, u32[]{:S(2)}) async-start(bf16[4,2,160,384]{2,0,1,3:T(4,128)(2,1)} %copy.92), calls=%async_computation | async-start | bytes 3145728 | tf_op jit(solution)/shard_map/all_to_all | solution.py:168
  91.3 1.6 fusion.40
  93.4 0.6 pad.17.clone
  94.3 7.1 %fusion.41 = f32[1,2,8,21,384]{4,2,3,1,0:T(8,128)S(1)} fusion(bf16[3,3,3,384,384]{4,3,2,1,0:T(8,128)(2,1)} %bitcast.52, bf16[3,4,1,7,2,384]{5,3,4,1,0,2:T(8,128)(2,1)S(1)} %slice.34, bf16[3,4,1,8,21,384]{5,3,4,1,0,2:T(8,128)(2,1)S(1)} %copy.89, pred[8,21]{0,1:T(8,128)(4,1)S(1)} %copy-done.7), kind=kOutput, calls=%fused_computation.59 | convolution fusion | flops 2680657920 | bytes 10156200 | tf_op jit(solution)/shard_map/conv_general_dilated | solution.py:56
  102.7 9.1 %all-to-all-done = bf16[4,2,160,384]{2,0,1,3:T(4,128)(2,1)S(1)} async-done(((bf16[4,2,160,384]{2,0,1,3:T(4,128)(2,1)}), bf16[4,2,160,384]{2,0,1,3:T(4,128)(2,1)S(1)}, u32[]{:S(2)}, u32[]{:S(2)}) %all-to-all-start) | async-done | bytes 983072 | tf_op jit(solution)/shard_map/all_to_all | solution.py:168
  111.7 2.5 %copy.94 = bf16[4,4,2,160,96]{4,3,2,1,0:T(8,128)(2,1)} copy(bf16[4,4,2,160,96]{3,0,2,4,1:T(4,128)(2,1)S(1)} %bitcast.46) | data formatting | bytes 1966080 | tf_op jit(solution)/shard_map/all_to_all | solution.py:168
  114.3 1.7 fusion.62
  116.3 0.8 copy-done.3
  117.5 1.6 fusion.20
  119.2 5.8 %fusion.10 = bf16[6,10,162,384]{3,2,1,0:T(8,128)(2,1)S(1)} fusion(bf16[4,4,160,384]{3,2,1,0:T(8,128)(2,1)S(1)} %get-tuple-element.16, bf16[4,4,160,384]{3,2,1,0:T(8,128)(2,1)S(1)} %get-tuple-element.15), kind=kLoop, calls=%fused_computation.15 | loop fusion | flops 70917120 | bytes 11397120 | tf_op jit(solution)/shard_map/concatenate | solution.py:135
  125.8 0.6 pad.15.clone
  127.1 3.8 %fusion.44 = f32[1,2,8,21,384]{4,2,3,1,0:T(8,128)S(1)} fusion(bf16[3,3,3,384,384]{4,3,2,1,0:T(8,128)(2,1)S(1)} %bitcast.55, bf16[3,4,1,7,2,384]{5,3,4,1,0,2:T(8,128)(2,1)S(1)} %slice.31, bf16[3,4,1,8,21,384]{5,3,4,1,0,2:T(8,128)(2,1)S(1)} %copy.84, pred[8,21]{0,1:T(8,128)(4,1)S(1)} %copy-done.7), kind=kOutput, calls=%fused_computation.60 | convolution fusion | flops 2680657920 | bytes 10156200 | tf_op jit(solution)/shard_map/conv_general_dilated | solution.py:43
  131.2 1.0 slice.32
  132.1 0.6 dynamic-slice_bitcast_fusion
  132.8 0.7 copy-done.4
  133.5 74.5 %fusion.6 = f32[2,3,3,384,96]{3,4,2,1,0:T(8,128)S(1)} fusion(bf16[5,10,162,384,1]{3,2,1,0,4:T(8,128)(2,1)S(1)} %dynamic-slice_bitcast_fusion, bf16[4,8,160,1,96]{4,2,1,0,3:T(8,128)(2,1)S(1)} %bitcast.51), kind=kOutput, calls=%fused_computation.11 | convolution fusion | flops 6794772480 | bytes 9858048 | tf_op jit(solution)/shard_map/conv_general_dilated | solution.py:95
  207.9 1.8 copy.97
  209.8 2.8 %reshape.42 = f32[6912,96]{0,1:T(8,128)} reshape(f32[2,3,3,384,96]{3,2,1,0,4:T(4,128)S(1)} %copy.97) | data formatting | bytes 5308416 | tf_op jit(solution)/shard_map/reshape | solution.py:102
  212.6 2.5 %dynamic-slice_multiply_fusion = f32[2592,96]{0,1:T(8,128)} fusion(f32[6912,96]{0,1:T(8,128)} %reshape.42, s32[]{:T(128)S(6)} %select_n.66), kind=kLoop, calls=%fused_computation.61 | loop fusion | flops 248832 | bytes 1990660 | tf_op jit(solution)/shard_map/mul | solution.py:179
  215.1 2.6 %add_convert_fusion = (bf16[1,2,160,384]{3,2,1,0:T(8,128)(2,1)}, bf16[1,2,160,384]{3,2,1,0:T(8,128)(2,1)}) fusion(bf16[1,2,160,384]{3,2,1,0:T(8,128)(2,1)} %param.9, f32[2,160]{1,0:T(2,128)S(1)} %broadcast_multiply_fusion, f32[2,160]{1,0:T(2,128)S(1)} %add_sqrt_fusion, f32[384]{0:T(512)S(1)} %copy-done.5, f32[1,2,1,160,384]{4,1,3,2,0:T(2,128)} %copy-done, ...), kind=kLoop, calls=%fused_computation.76 | loop fusion | flops 2580480 | bytes 1971712 | tf_op jit(solution)/shard_map/convert_element_type | solution.py:196
  (41 shorter events, 4.7 us)
Async XLA Ops:
  7.2 50.6 %all-gather.2.cloned.1.call-start = ((), (), s32[]{:S(2)}) async-start(), calls=%async_computation.1 | async-start | bytes 2457600 | tf_op jit(solution)/shard_map/all_gather | solution.py:162
  59.4 23.7 %collective-permute-start = (bf16[4,2,160,384]{3,2,1,0:T(8,128)(2,1)S(1)}, bf16[4,2,160,384]{3,2,1,0:T(8,128)(2,1)S(1)}, u32[]{:S(2)}, u32[]{:S(2)}) collective-permute-start(bf16[4,2,160,384]{3,2,1,0:T(8,128)(2,1)S(1)} %get-tuple-element.18), channel_id=1, source_target_pairs={{0,2},{1,3},{2,0},{3,1},{4,6},{5,7},{6,4},{7,5},{8,10},{9,11},{10,... | collective-permute-start | bytes 2949128 | tf_op jit(solution)/shard_map/ppermute | solution.py:115
  62.0 29.3 %collective-permute-start.3 = (bf16[3,1,160,384]{3,2,1,0:T(8,128)(2,1)}, bf16[3,1,160,384]{3,2,1,0:T(8,128)(2,1)}, u32[]{:S(2)}, u32[]{:S(2)}) collective-permute-start(bf16[3,1,160,384]{3,2,1,0:T(8,128)(2,1)} %get-tuple-element.22), channel_id=1, source_target_pairs={{1,0},{2,1},{3,2},{5,4},{6,5},{7,6},{9,8},{10,9},{11,10},{13,12},{... | collective-permute-start | bytes 1105928 | tf_op jit(solution)/shard_map/ppermute | solution.py:24
  63.3 28.0 %collective-permute-start.2 = (bf16[3,1,160,384]{3,2,1,0:T(8,128)(2,1)}, bf16[3,1,160,384]{3,2,1,0:T(8,128)(2,1)}, u32[]{:S(2)}, u32[]{:S(2)}) collective-permute-start(bf16[3,1,160,384]{3,2,1,0:T(8,128)(2,1)} %get-tuple-element.21), channel_id=1, source_target_pairs={{0,1},{1,2},{2,3},{4,5},{5,6},{6,7},{8,9},{9,10},{10,11},{12,13},{... | collective-permute-start | bytes 1105928 | tf_op jit(solution)/shard_map/ppermute | solution.py:22
  83.1 4.2 %copy-start.2 = (bf16[4,2,160,384]{3,2,1,0:T(8,128)(2,1)}, bf16[4,2,160,384]{3,2,1,0:T(8,128)(2,1)S(1)}, u32[]{:S(2)}) copy-start(bf16[4,2,160,384]{3,2,1,0:T(8,128)(2,1)S(1)} %collective-permute-done) | copy-start | bytes 2949124
  84.7 29.5 %collective-permute-start.1 = (bf16[4,4,160,384]{3,2,1,0:T(8,128)(2,1)}, bf16[4,4,160,384]{3,2,1,0:T(8,128)(2,1)}, u32[]{:S(2)}, u32[]{:S(2)}) collective-permute-start(bf16[4,4,160,384]{3,2,1,0:T(8,128)(2,1)} %pad_maximum_fusion.1), channel_id=1, source_target_pairs={{0,1},{1,0},{2,3},{3,2},{4,5},{5,4},{6,7},{7,6},{8,9},{9,8},{10,11... | collective-permute-start | bytes 5898248 | tf_op jit(solution)/shard_map/ppermute | solution.py:121
  87.3 24.4 %all-to-all-start = ((bf16[4,2,160,384]{2,0,1,3:T(4,128)(2,1)}), bf16[4,2,160,384]{2,0,1,3:T(4,128)(2,1)S(1)}, u32[]{:S(2)}, u32[]{:S(2)}) async-start(bf16[4,2,160,384]{2,0,1,3:T(4,128)(2,1)} %copy.92), calls=%async_computation | async-start | bytes 3145728 | tf_op jit(solution)/shard_map/all_to_all | solution.py:168
  93.4 0.9 copy-start.7
  94.3 7.6 %copy-start.1 = (bf16[1,2,160,384]{3,2,1,0:T(8,128)(2,1)S(1)}, bf16[1,2,160,384]{3,2,1,0:T(8,128)(2,1)}, u32[]{:S(2)}) copy-start(bf16[1,2,160,384]{3,2,1,0:T(8,128)(2,1)} %param.5) | copy-start | bytes 737284
  94.3 7.6 %copy-start.5 = (f32[384]{0:T(512)S(1)}, f32[384]{0:T(512)}, u32[]{:S(2)}) copy-start(f32[384]{0:T(512)} %param.6) | copy-start | bytes 4612
  101.9 0.8 copy-start
  116.0 1.2 copy-start.3
  119.2 7.5 %slice-start = ((s8[7962624]{0:T(1024)(128)(4,1)}), s8[4194304]{0:T(1024)(128)(4,1)S(1)}, s32[]{:S(2)}) async-start(s8[7962624]{0:T(1024)(128)(4,1)} %bitcast.53), calls=%async_computation.2 | async-start | bytes 8388608
  125.0 2.1 slice-start.1
  132.1 1.3 copy-start.4
  209.7 5.3 %copy-start.6 = (f32[384]{0:T(512)S(1)}, f32[384]{0:T(512)}, u32[]{:S(2)}) copy-start(f32[384]{0:T(512)} %param.7) | copy-start | bytes 4612
Sparse Core Ops, SparseCore 0:
  11.4 46.2 all-gather.1
where the time goes:
time: 225 us; the launch traced here: 224 us
  matrix products  85.4 us (38%)
  waiting for transfers between devices  71.6 us (32%)
  local copies, waits for them, and re-layouts  21.8 us (10%)
  other arithmetic  20.9 us (9%)
  between operations  14.3 us (6%)
  starting transfers between devices  10.5 us (5%)
    conv_general_dilated x1, matrix products, block_weight_grad(): lax.conv_general_dilated(frames[..., None], cot_all[:, :, :, None, :], (1...  74.5 us
    all_gather x1, waiting for transfers between devices, local(): lax.all_gather(jnp.concatenate([hidden, cotangent], axis=-1), 'tm', axis=...  46.4 us
    ppermute x1, waiting for transfers between devices, gather_rows(): lax.ppermute(own, 'height', [(i, (i + 2 * step) % height_count) for i in...  16.1 us
    all_to_all x1, waiting for transfers between devices, local(): lax.all_to_all(cot_frames, 'height', split_axis=3, concat_axis=1, tiled=T...  9.06 us
    conv_general_dilated x1, matrix products, backward_conv(): lax.conv_general_dilated(window[None], jnp.flip(cube, (0, 1, 2)), (1, 1,...  7.08 us
    concatenate x1, other arithmetic, gather_rows(): jnp.concatenate([lax.dynamic_slice_in_dim(relative, (place - chip - 1) %...  5.81 us
  transfers between devices with their start and end apart: 6, of which 3 were waited for; matrix products, arithmetic and copies ran while one was open for 8% of the time, Pallas kernels for 0%

commit v1 on v0

--- a/solution.py
+++ b/solution.py
@@ -3,6 +3,12 @@
 import jax.numpy as jnp
 from jax import lax
 from jax.sharding import PartitionSpec as P
+
+
+def laid_out(parts, dim):
+    shape = list(parts.shape[1:])
+    shape[dim] *= parts.shape[0]
+    return jnp.moveaxis(parts, 0, dim).reshape(shape)
 
 
 def shifted_2(value, axis, by):
@@ -159,9 +165,15 @@
     right_pad = padded_cols - col_count - 1
     inverse_root = 1.0 / math.sqrt(total_frames * total_rows * col_count)
     weight_cube = weight.reshape(3, 3, 3, channels, channels)
-    both_frames = lax.all_gather(
-        jnp.concatenate([hidden, cotangent], axis=-1), "tm", axis=0, tiled=True
-    )
+    x = jnp.concatenate([hidden, cotangent], axis=-1)
+    peers = lax.axis_size("tm")
+    ahead = [(i_2, (i_2 + 1) % peers) for i_2 in range(peers)]
+    blocks = [x]
+    while len(blocks) < peers:
+        blocks.append(lax.ppermute(blocks[-1], "tm", ahead))
+    index_2 = lax.axis_index("tm")
+    blocks = jnp.stack(blocks)[(index_2 - jnp.arange(peers)) % peers]
+    both_frames = laid_out(blocks, 0)
     hidden_all = gather_rows(both_frames[..., :channels], height_count)
     framed = jnp.pad(hidden_all, ((2, 0), (1, 1), (1, right_pad), (0, 0)))
     cot_frames = both_frames[..., channels:]

time: 225 us -> 210 us (0.933)
  between operations: 14.3 us -> 0.95 us
  waiting for transfers between devices: 71.6 us -> 65.4 us
  local copies, waits for them, and re-layouts: 21.8 us -> 24.7 us
  starting transfers between devices: 10.5 us -> 13.1 us
    all_gather x1 -> x0, waiting for transfers between devices: 46.4 us -> none  [local(): lax.all_gather(jnp.concatenate([hidden, cotangent], axis=-1), 'tm', axis=...]
    ppermute x0 -> x3, waiting for transfers between devices: none -> 40.8 us  [local(): blocks.append(lax.ppermute(blocks[-1], 'tm', ahead))]
    ppermute x0 -> x3, starting transfers between devices: none -> 3.08 us  [local(): blocks.append(lax.ppermute(blocks[-1], 'tm', ahead))]
    another operation x0 -> x2, other arithmetic: none -> 2.29 us  [local(): blocks = jnp.stack(blocks)[(index_2 - jnp.arange(peers)) % peers]]
  transfers between devices with their start and end apart: 6 -> 8, of which waited for: 3 -> 5; matrix products, arithmetic and copies ran while one was open for 8% -> 9% of each run, Pallas kernels for 0% -> 0%
where the time goes in v1:
time: 210 us
  matrix products  85.3 us (41%)
  waiting for transfers between devices  65.4 us (31%)
  local copies, waits for them, and re-layouts  24.7 us (12%)
  other arithmetic  20.2 us (10%)
  starting transfers between devices  13.1 us (6%)
    conv_general_dilated x1, matrix products, block_weight_grad(): lax.conv_general_dilated(frames[..., None], cot_all[:, :, :, None, :], (1...  74.5 us
    ppermute x3, waiting for transfers between devices, local(): blocks.append(lax.ppermute(blocks[-1], 'tm', ahead))  40.8 us
    ppermute x1, waiting for transfers between devices, gather_rows(): lax.ppermute(own, 'height', [(i, (i + 2 * step) % height_count) for i in...  16.1 us
    all_to_all x1, waiting for transfers between devices, local(): lax.all_to_all(cot_frames, 'height', split_axis=3, concat_axis=1, tiled=T...  8.42 us
    conv_general_dilated x1, matrix products, backward_conv(): lax.conv_general_dilated(window[None], jnp.flip(cube, (0, 1, 2)), (1, 1,...  7.03 us
    concatenate x1, other arithmetic, gather_rows(): jnp.concatenate([lax.dynamic_slice_in_dim(relative, (place - chip - 1) %...  5.85 us
    unnamed x30, local copies, waits for them, and re-layouts  4.43 us
    slice x2, local copies, waits for them, and re-layouts, local(): cot_frames = both_frames[..., channels:]  4.23 us
  transfers between devices with their start and end apart: 8, of which 5 were waited for; matrix products, arithmetic and copies ran while one was open for 9% of the time, Pallas kernels for 0%

profile of v1, /device:TPU:0, one launch (start us, length us, event | category | flops | bytes accessed | tf_op | source)
XLA Modules:
  0.0 209.7 jit_solution(8369568163339255158)
XLA Ops:
  0.6 1.1 fusion.49
  1.7 1.2 multiply_convert_fusion
  3.0 1.0 fusion.63
  4.0 3.1 %collective-permute-start = (bf16[1,2,160,768]{3,2,1,0:T(8,128)(2,1)S(1)}, bf16[1,2,160,768]{3,2,1,0:T(8,128)(2,1)S(1)}, u32[]{:S(2)}, u32[]{:S(2)}) collective-permute-start(bf16[1,2,160,768]{3,2,1,0:T(8,128)(2,1)S(1)} %get-tuple-element.24), channel_id=1, source_target_pairs={{0,4},{4,8},{8,12},{12,0},{1,5},{5,9},{9,13},{13,1},{2,6},{6,10},{... | collective-permute-start | bytes 1474568 | tf_op jit(solution)/shard_map/ppermute | solution.py:173
  7.0 13.2 %collective-permute-done = bf16[1,2,160,768]{3,2,1,0:T(8,128)(2,1)S(1)} collective-permute-done((bf16[1,2,160,768]{3,2,1,0:T(8,128)(2,1)S(1)}, bf16[1,2,160,768]{3,2,1,0:T(8,128)(2,1)S(1)}, u32[]{:S(2)}, u32[]{:S(2)}) %collective-permute-start) | collective-permute-done | bytes 491552 | tf_op jit(solution)/shard_map/ppermute | solution.py:173
  20.3 14.2 %collective-permute-done.1 = bf16[1,2,160,768]{3,2,1,0:T(8,128)(2,1)S(1)} collective-permute-done((bf16[1,2,160,768]{3,2,1,0:T(8,128)(2,1)S(1)}, bf16[1,2,160,768]{3,2,1,0:T(8,128)(2,1)S(1)}, u32[]{:S(2)}, u32[]{:S(2)}) %collective-permute-start.1) | collective-permute-done | bytes 491552 | tf_op jit(solution)/shard_map/ppermute | solution.py:173
  34.5 13.4 %collective-permute-done.2 = bf16[1,2,160,768]{3,2,1,0:T(8,128)(2,1)} collective-permute-done((bf16[1,2,160,768]{3,2,1,0:T(8,128)(2,1)S(1)}, bf16[1,2,160,768]{3,2,1,0:T(8,128)(2,1)}, u32[]{:S(2)}, u32[]{:S(2)}) %collective-permute-start.2) | collective-permute-done | bytes 491552 | tf_op jit(solution)/shard_map/ppermute | solution.py:173
  47.9 1.3 maximum_bitcast_fusion
  49.2 2.0 gather_fusion
  51.1 1.7 fusion.64
  52.8 1.1 collective-permute-start.3
  53.9 1.0 pad_dynamic-slice_fusion.5
  54.9 1.3 collective-permute-start.6
  56.2 3.8 %collective-permute-start.5 = (bf16[3,1,160,384]{3,2,1,0:T(8,128)(2,1)}, bf16[3,1,160,384]{3,2,1,0:T(8,128)(2,1)}, u32[]{:S(2)}, u32[]{:S(2)}) collective-permute-start(bf16[3,1,160,384]{3,2,1,0:T(8,128)(2,1)} %get-tuple-element.21), channel_id=1, source_target_pairs={{0,1},{1,2},{2,3},{4,5},{5,6},{6,7},{8,9},{9,10},{10,11},{12,13},{... | collective-permute-start | bytes 1105928 | tf_op jit(solution)/shard_map/ppermute | solution.py:28
  60.0 16.1 %collective-permute-done.3 = bf16[4,2,160,384]{3,2,1,0:T(8,128)(2,1)S(1)} collective-permute-done((bf16[4,2,160,384]{3,2,1,0:T(8,128)(2,1)S(1)}, bf16[4,2,160,384]{3,2,1,0:T(8,128)(2,1)S(1)}, u32[]{:S(2)}, u32[]{:S(2)}) %collective-permute-start.3) | collective-permute-done | bytes 983072 | tf_op jit(solution)/shard_map/ppermute | solution.py:121
  76.1 1.6 pad_maximum_fusion.1
  77.8 2.5 %copy.114 = bf16[4,2,160,384]{2,0,1,3:T(4,128)(2,1)} copy(bf16[4,2,160,384]{3,2,1,0:T(8,128)(2,1)S(1)} %get-tuple-element.17) | data formatting | bytes 1966080 | tf_op jit(solution)/shard_map/slice | solution.py:179
  80.3 3.9 %all-to-all-start = ((bf16[4,2,160,384]{2,0,1,3:T(4,128)(2,1)}), bf16[4,2,160,384]{2,0,1,3:T(4,128)(2,1)S(1)}, u32[]{:S(2)}, u32[]{:S(2)}) async-start(bf16[4,2,160,384]{2,0,1,3:T(4,128)(2,1)} %copy.114), calls=%async_computation | async-start | bytes 3145728 | tf_op jit(solution)/shard_map/all_to_all | solution.py:180
  84.3 1.6 fusion.40
  87.7 7.0 %fusion.41 = f32[1,2,8,21,384]{4,2,3,1,0:T(8,128)S(1)} fusion(bf16[3,3,3,384,384]{4,3,2,1,0:T(8,128)(2,1)} %bitcast.63, bf16[3,4,1,7,2,384]{5,3,4,1,0,2:T(8,128)(2,1)S(1)} %slice.36, bf16[3,4,1,8,21,384]{5,3,4,1,0,2:T(8,128)(2,1)S(1)} %copy.111, pred[8,21]{0,1:T(8,128)(4,1)S(1)} %copy-done.11), kind=kOutput, calls=%fused_computation.61 | convolution fusion | flops 2680657920 | bytes 10156200 | tf_op jit(solution)/shard_map/conv_general_dilated | solution.py:62
  96.5 8.4 %all-to-all-done = bf16[4,2,160,384]{2,0,1,3:T(4,128)(2,1)S(1)} async-done(((bf16[4,2,160,384]{2,0,1,3:T(4,128)(2,1)}), bf16[4,2,160,384]{2,0,1,3:T(4,128)(2,1)S(1)}, u32[]{:S(2)}, u32[]{:S(2)}) %all-to-all-start) | async-done | bytes 983072 | tf_op jit(solution)/shard_map/all_to_all | solution.py:180
  104.9 2.5 %copy.116 = bf16[4,4,2,160,96]{4,3,2,1,0:T(8,128)(2,1)} copy(bf16[4,4,2,160,96]{3,0,2,4,1:T(4,128)(2,1)S(1)} %bitcast.55) | data formatting | bytes 1966080 | tf_op jit(solution)/shard_map/all_to_all | solution.py:180
  107.5 1.7 fusion.65
  110.7 1.6 fusion.20
  112.4 5.9 %fusion.10 = bf16[6,10,162,384]{3,2,1,0:T(8,128)(2,1)S(1)} fusion(bf16[4,4,160,384]{3,2,1,0:T(8,128)(2,1)S(1)} %get-tuple-element.16, bf16[4,4,160,384]{3,2,1,0:T(8,128)(2,1)S(1)} %get-tuple-element.15), kind=kLoop, calls=%fused_computation.16 | loop fusion | flops 70917120 | bytes 11397120 | tf_op jit(solution)/shard_map/concatenate | solution.py:141
  120.3 3.8 %fusion.44 = f32[1,2,8,21,384]{4,2,3,1,0:T(8,128)S(1)} fusion(bf16[3,3,3,384,384]{4,3,2,1,0:T(8,128)(2,1)S(1)} %bitcast.66, bf16[3,4,1,7,2,384]{5,3,4,1,0,2:T(8,128)(2,1)S(1)} %slice.33, bf16[3,4,1,8,21,384]{5,3,4,1,0,2:T(8,128)(2,1)S(1)} %copy.106, pred[8,21]{0,1:T(8,128)(4,1)S(1)} %copy-done.11), kind=kOutput, calls=%fused_computation.62 | convolution fusion | flops 2680657920 | bytes 10156200 | tf_op jit(solution)/shard_map/conv_general_dilated | solution.py:49
  124.4 1.0 slice.34
  126.7 74.5 %fusion.6 = f32[2,3,3,384,96]{3,4,2,1,0:T(8,128)S(1)} fusion(bf16[5,10,162,384,1]{3,2,1,0,4:T(8,128)(2,1)S(1)} %dynamic-slice_bitcast_fusion, bf16[4,8,160,1,96]{4,2,1,0,3:T(8,128)(2,1)S(1)} %bitcast.60), kind=kOutput, calls=%fused_computation.12 | convolution fusion | flops 6794772480 | bytes 9858048 | tf_op jit(solution)/shard_map/conv_general_dilated | solution.py:101
  201.1 1.8 copy.119
  203.0 2.8 %reshape.95 = f32[6912,96]{0,1:T(8,128)} reshape(f32[2,3,3,384,96]{3,2,1,0,4:T(4,128)S(1)} %copy.119) | data formatting | bytes 5308416 | tf_op jit(solution)/shard_map/reshape | solution.py:108
  205.8 2.6 %dynamic-slice_multiply_fusion = f32[2592,96]{0,1:T(8,128)} fusion(f32[6912,96]{0,1:T(8,128)} %reshape.95, s32[]{:T(128)S(6)} %select_n.91), kind=kLoop, calls=%fused_computation.63 | loop fusion | flops 248832 | bytes 1990660 | tf_op jit(solution)/shard_map/mul | solution.py:191
  208.5 1.2 add_convert_fusion
  (56 shorter events, 8.8 us)
Async XLA Ops:
  4.0 16.3 %collective-permute-start = (bf16[1,2,160,768]{3,2,1,0:T(8,128)(2,1)S(1)}, bf16[1,2,160,768]{3,2,1,0:T(8,128)(2,1)S(1)}, u32[]{:S(2)}, u32[]{:S(2)}) collective-permute-start(bf16[1,2,160,768]{3,2,1,0:T(8,128)(2,1)S(1)} %get-tuple-element.24), channel_id=1, source_target_pairs={{0,4},{4,8},{8,12},{12,0},{1,5},{5,9},{9,13},{13,1},{2,6},{6,10},{... | collective-permute-start | bytes 1474568 | tf_op jit(solution)/shard_map/ppermute | solution.py:173
  20.3 14.2 %collective-permute-start.1 = (bf16[1,2,160,768]{3,2,1,0:T(8,128)(2,1)S(1)}, bf16[1,2,160,768]{3,2,1,0:T(8,128)(2,1)S(1)}, u32[]{:S(2)}, u32[]{:S(2)}) collective-permute-start(bf16[1,2,160,768]{3,2,1,0:T(8,128)(2,1)S(1)} %collective-permute-done), channel_id=1, source_target_pairs={{0,4},{4,8},{8,12},{12,0},{1,5},{5,9},{9,13},{13,1},{2,6},{6,10},{... | collective-permute-start | bytes 1474568 | tf_op jit(solution)/shard_map/ppermute | solution.py:173
  34.5 13.4 %collective-permute-start.2 = (bf16[1,2,160,768]{3,2,1,0:T(8,128)(2,1)S(1)}, bf16[1,2,160,768]{3,2,1,0:T(8,128)(2,1)}, u32[]{:S(2)}, u32[]{:S(2)}) collective-permute-start(bf16[1,2,160,768]{3,2,1,0:T(8,128)(2,1)S(1)} %collective-permute-done.1), channel_id=1, source_target_pairs={{0,4},{4,8},{8,12},{12,0},{1,5},{5,9},{9,13},{13,1},{2,6},{6,10},{... | collective-permute-start | bytes 1474568 | tf_op jit(solution)/shard_map/ppermute | solution.py:173
  52.8 23.3 %collective-permute-start.3 = (bf16[4,2,160,384]{3,2,1,0:T(8,128)(2,1)S(1)}, bf16[4,2,160,384]{3,2,1,0:T(8,128)(2,1)S(1)}, u32[]{:S(2)}, u32[]{:S(2)}) collective-permute-start(bf16[4,2,160,384]{3,2,1,0:T(8,128)(2,1)S(1)} %get-tuple-element.18), channel_id=1, source_target_pairs={{0,2},{1,3},{2,0},{3,1},{4,6},{5,7},{6,4},{7,5},{8,10},{9,11},{10,... | collective-permute-start | bytes 2949128 | tf_op jit(solution)/shard_map/ppermute | solution.py:121
  54.9 29.4 %collective-permute-start.6 = (bf16[3,1,160,384]{3,2,1,0:T(8,128)(2,1)}, bf16[3,1,160,384]{3,2,1,0:T(8,128)(2,1)}, u32[]{:S(2)}, u32[]{:S(2)}) collective-permute-start(bf16[3,1,160,384]{3,2,1,0:T(8,128)(2,1)} %get-tuple-element.22), channel_id=1, source_target_pairs={{1,0},{2,1},{3,2},{5,4},{6,5},{7,6},{9,8},{10,9},{11,10},{13,12},{... | collective-permute-start | bytes 1105928 | tf_op jit(solution)/shard_map/ppermute | solution.py:30
  56.2 28.1 %collective-permute-start.5 = (bf16[3,1,160,384]{3,2,1,0:T(8,128)(2,1)}, bf16[3,1,160,384]{3,2,1,0:T(8,128)(2,1)}, u32[]{:S(2)}, u32[]{:S(2)}) collective-permute-start(bf16[3,1,160,384]{3,2,1,0:T(8,128)(2,1)} %get-tuple-element.21), channel_id=1, source_target_pairs={{0,1},{1,2},{2,3},{4,5},{5,6},{6,7},{8,9},{9,10},{10,11},{12,13},{... | collective-permute-start | bytes 1105928 | tf_op jit(solution)/shard_map/ppermute | solution.py:28
  76.1 1.6 copy-start.4
  77.7 29.7 %collective-permute-start.4 = (bf16[4,4,160,384]{3,2,1,0:T(8,128)(2,1)}, bf16[4,4,160,384]{3,2,1,0:T(8,128)(2,1)}, u32[]{:S(2)}, u32[]{:S(2)}) collective-permute-start(bf16[4,4,160,384]{3,2,1,0:T(8,128)(2,1)} %pad_maximum_fusion.1), channel_id=1, source_target_pairs={{0,1},{1,0},{2,3},{3,2},{4,5},{5,4},{6,7},{7,6},{8,9},{9,8},{10,11... | collective-permute-start | bytes 5898248 | tf_op jit(solution)/shard_map/ppermute | solution.py:127
  80.3 24.6 %all-to-all-start = ((bf16[4,2,160,384]{2,0,1,3:T(4,128)(2,1)}), bf16[4,2,160,384]{2,0,1,3:T(4,128)(2,1)S(1)}, u32[]{:S(2)}, u32[]{:S(2)}) async-start(bf16[4,2,160,384]{2,0,1,3:T(4,128)(2,1)} %copy.114), calls=%async_computation | async-start | bytes 3145728 | tf_op jit(solution)/shard_map/all_to_all | solution.py:180
  87.0 0.7 copy-start.11
  94.8 0.9 copy-start.2
  94.8 0.9 copy-start.9
  95.7 0.8 copy-start
  109.2 1.2 copy-start.5
  112.3 7.5 %slice-start = ((s8[7962624]{0:T(1024)(128)(4,1)}), s8[4194304]{0:T(1024)(128)(4,1)S(1)}, s32[]{:S(2)}) async-start(s8[7962624]{0:T(1024)(128)(4,1)} %bitcast.64), calls=%async_computation.1 | async-start | bytes 8388608
  118.2 2.1 slice-start.1
  125.4 1.3 copy-start.7
  205.8 2.7 %copy-start.1 = (f32[1,2,1,160,384]{4,1,3,2,0:T(2,128)S(1)}, f32[1,2,1,160,384]{4,1,3,2,0:T(2,128)}, u32[]{:S(2)}) copy-start(f32[1,2,1,160,384]{4,1,3,2,0:T(2,128)} %copy-done) | copy-start | bytes 1474564
  205.8 2.7 %copy-start.3 = (bf16[1,2,160,384]{3,2,1,0:T(8,128)(2,1)S(1)}, bf16[1,2,160,384]{3,2,1,0:T(8,128)(2,1)}, u32[]{:S(2)}) copy-start(bf16[1,2,160,384]{3,2,1,0:T(8,128)(2,1)} %param.5) | copy-start | bytes 737284
  205.8 2.7 %copy-start.6 = (f32[1,2,1,160,384]{4,1,3,2,0:T(2,128)S(1)}, f32[1,2,1,160,384]{4,1,3,2,0:T(2,128)}, u32[]{:S(2)}) copy-start(f32[1,2,1,160,384]{4,1,3,2,0:T(2,128)} %slice.34) | copy-start | bytes 1474564
  205.8 2.7 %copy-start.8 = (bf16[1,2,160,384]{3,2,1,0:T(8,128)(2,1)S(1)}, bf16[1,2,160,384]{3,2,1,0:T(8,128)(2,1)}, u32[]{:S(2)}) copy-start(bf16[1,2,160,384]{3,2,1,0:T(8,128)(2,1)} %param.9) | copy-start | bytes 737284
  205.8 2.7 %copy-start.10 = (f32[384]{0:T(512)S(1)}, f32[384]{0:T(512)}, u32[]{:S(2)}) copy-start(f32[384]{0:T(512)} %param.7) | copy-start | bytes 4612
